TPU v7x, 128 devices: a whole 4x4x4 slice. The times are simulated.
128 devices in a mesh: grp: 8 (over z, core), dev: 16 (over y, x).
Axes of the slice: x: 4, y: 4, z: 4, core: 2. Of those that a mesh axis runs over, the one named last changes fastest.
Arguments:
- positions: float32 [3, 131072], P(None, ('grp', 'dev')), may hold values from -3 to 3
- velocities: float32 [3, 131072], P(None, ('grp', 'dev')), may hold values from -5 to 5
- accelerations: float32 [3, 131072], P(None, ('grp', 'dev')), may hold values from -3 to 3
- jerks: float32 [3, 131072], P(None, ('grp', 'dev')), may hold values from -3 to 3
- levels: int32 [131072], P(('grp', 'dev')), may hold values from 0 to 5
- counts: int32 [2, 128], replicated, may hold values from 1 to 256, 16384 in all within a row
- active_rows: int32 [2, 32768], P(None, ('grp', 'dev')), may hold values from 0 to 1023, as said below
Outputs:
- new_positions: float32 [3, 131072], P(None, ('grp', 'dev'))
- new_velocities: float32 [3, 131072], P(None, ('grp', 'dev'))
- new_accelerations: float32 [3, 131072], P(None, ('grp', 'dev'))
- new_jerks: float32 [3, 131072], P(None, ('grp', 'dev'))
Inputs may be any that keep to these rules, and one draw needn't show every extreme that they name: In each step the 128 counts sum to exactly 16384 and the largest of them is exactly 256. `active_rows`: for each step and device, the 256 entries of the device's slots are distinct indices of that device's own stars; only the first counts of them are live.
All inputs are finite; a program needn't handle non-finite values.
Results may differ from a plain program's by a relative error of at most 0.00022.
Values sent between devices are 32-bit elements; how exact they have to be, the bound alone decides.
No kernel may reach another device: no remote copies, remote signals or barrier semaphores. Data moves between devices by JAX's collectives and lax.ppermute only.
A program may use at most 128 MiB of HBM per device.

v0:
```python
import math
import jax
import jax.numpy as jnp
from jax import lax
from jax.sharding import PartitionSpec as P

tick_length = 1.0 / 128.0


def pair_block(targets, src_pos, src_vel, mass, soft_sq):
    gap_x = src_pos[0][None, :] - targets[0][:, None]
    gap_y = src_pos[1][None, :] - targets[1][:, None]
    gap_z = src_pos[2][None, :] - targets[2][:, None]
    drift_x = src_vel[0][None, :] - targets[3][:, None]
    drift_y = src_vel[1][None, :] - targets[4][:, None]
    drift_z = src_vel[2][None, :] - targets[5][:, None]
    squared = gap_x * gap_x + gap_y * gap_y + gap_z * gap_z + soft_sq
    inverse = lax.rsqrt(squared)
    weight = mass * inverse * inverse * inverse
    along = 3.0 * (gap_x * drift_x + gap_y * drift_y + gap_z * drift_z) * inverse * inverse
    return jnp.stack(
        [
            jnp.sum(weight * gap_x, axis=1),
            jnp.sum(weight * gap_y, axis=1),
            jnp.sum(weight * gap_z, axis=1),
            jnp.sum(weight * (drift_x - along * gap_x), axis=1),
            jnp.sum(weight * (drift_y - along * gap_y), axis=1),
            jnp.sum(weight * (drift_z - along * gap_z), axis=1),
        ]
    )


def block_terms(packed, src_pos, src_vel, mass, soft_sq):
    width, total = packed.shape
    block = math.gcd(total, 2048)
    grouped = packed.reshape(width, total // block, block).transpose(1, 0, 2)
    result = lax.map(lambda targets: pair_block(targets, src_pos, src_vel, mass, soft_sq), grouped)
    return result.transpose(1, 0, 2).reshape(width, total)


def predict(positions, velocities, accelerations, jerks, elapsed):
    span = elapsed[None, :]
    pred_pos = (
        positions
        + span * velocities
        + 0.5 * span * span * accelerations
        + span * span * span / 6.0 * jerks
    )
    pred_vel = velocities + span * accelerations + 0.5 * span * span * jerks
    return (pred_pos, pred_vel)


def correct(old_pos, old_vel, old_acc, old_jerk, force, jerk_new, span):
    span = span[None, :]
    new_vel = old_vel + 0.5 * span * (old_acc + force) + span * span / 12.0 * (old_jerk - jerk_new)
    new_pos = old_pos + 0.5 * span * (old_vel + new_vel) + span * span / 12.0 * (old_acc - force)
    return (new_pos, new_vel)


def shards(positions, velocities, accelerations, jerks, levels, counts, active_rows):
    devices_all = lax.axis_size("grp") * lax.axis_size("dev")
    my_rank = lax.axis_index("grp") * lax.axis_size("dev") + lax.axis_index("dev")
    star_dev = positions.shape[1]
    slot_cap = active_rows.shape[1]
    stars_all = star_dev * devices_all
    mass = 1.0 / stars_all
    soft_sq = 0.0004 * (131072.0 / stars_all) ** (2.0 / 3.0)
    last_time = -(jnp.left_shift(jnp.int32(1), levels) - 1).astype(jnp.float32) * tick_length
    for step in range(active_rows.shape[0]):
        now = (step + 1) * tick_length
        pred_pos, pred_vel = predict(positions, velocities, accelerations, jerks, now - last_time)
        rows = active_rows[step]
        targets = jnp.concatenate([pred_pos[:, rows], pred_vel[:, rows]], axis=0)
        step_counts = counts[step]
        own_count = step_counts[my_rank]
        gathered = lax.all_gather(targets[None], ("grp", "dev"), axis=0, tiled=True)
        flat = gathered.transpose(1, 0, 2).reshape(6, devices_all * slot_cap)
        terms = block_terms(flat, pred_pos, pred_vel, mass, soft_sq)
        totals = lax.psum(terms, ("grp", "dev"))
        own = lax.dynamic_slice_in_dim(totals, my_rank * slot_cap, slot_cap, 1)
        span = now - last_time[rows]
        new_pos, new_vel = correct(
            positions[:, rows],
            velocities[:, rows],
            accelerations[:, rows],
            jerks[:, rows],
            own[:3],
            own[3:],
            span,
        )
        live = jnp.arange(slot_cap, dtype=jnp.int32) < own_count
        target = jnp.where(live, rows, star_dev)
        positions = positions.at[:, target].set(new_pos, mode="drop")
        velocities = velocities.at[:, target].set(new_vel, mode="drop")
        accelerations = accelerations.at[:, target].set(own[:3], mode="drop")
        jerks = jerks.at[:, target].set(own[3:], mode="drop")
        last_time = last_time.at[target].set(now, mode="drop")
    return (positions, velocities, accelerations, jerks)


def solution(mesh):
    placed = (
        P(None, ("grp", "dev")),
        P(None, ("grp", "dev")),
        P(None, ("grp", "dev")),
        P(None, ("grp", "dev")),
        P(("grp", "dev")),
        P(),
        P(None, ("grp", "dev")),
    )
    return jax.shard_map(
        shards,
        mesh=mesh,
        in_specs=placed,
        out_specs=(
            P(None, ("grp", "dev")),
            P(None, ("grp", "dev")),
            P(None, ("grp", "dev")),
            P(None, ("grp", "dev")),
        ),
        check_vma=False,
    )
```

profile of v0, /device:TPU:1, one launch (start us, length us, event | category | flops | bytes accessed | tf_op | source)
XLA Modules:
  0.0 1007.9 jit_solution(7098034643428185469)
XLA Ops:
  14.2 63.9 %all-gather.2 = f32[128,6,256]{2,1,0:T(8,128)S(1)} all-gather(f32[1,6,256]{2,1,0:T(8,128)S(1)} %maximum_bitcast_fusion), channel_id=2, replica_groups=mesh['grp'=8,'dev'=16] {'grp','dev'}, dimensions={0}, use_global_device_ids=true | all-gather | bytes 792576 | tf_op jit(solution)/shard_map/all_gather | solution.py:76
  78.2 263.2 %while.20 = (s32[]{:T(128)}, f32[16,6,2048]{2,1,0:T(8,128)S(1)}, f32[3,1024]{1,0:T(4,128)S(1)}, f32[16,6,2048]{2,1,0:T(8,128)S(1)}, f32[3,1024]{1,0:T(4,128)S(1)...) while((s32[]{:T(128)}, f32[16,6,2048]{2,1,0:T(8,128)S(1)}, ...), condition=%wide.region_7.8_spmd, body=%wide.region_0.7_spmd.sunk | while | flops 85970952 | bytes 499917 | solution.py:37
  78.3 16.2 %fusion.64 = (f32[2048]{0:T(1024)S(1)}, f32[2048]{0:T(1024)S(1)}, f32[2048]{0:T(1024)S(1)}, f32[2048]{0:T(1024)S(1)}, f32[2048]{0:T(1024)S(1)}, /*index=5*/f32[2048]{0:T(1024)S(1)}) fusion(f32[2048]{0:T(1024)S(1)} %bitcast.257, f32[1024]{0:T(1024)S(1)} %bitcast.269, f32[2048]{0:T(1024)S(1)} %bitcast.254, f32[1024]{0:T(1024)S(1)} %bitcast.272, ...), kind=kLoop, calls=%fused_computation.45.clone.1 | loop fusion | flops 85970944 | bytes 122880 | tf_op jit(solution)/shard_map/while/body/eval_jaxpr/reduce_sum | solution.py:28
  94.8 16.2 %fusion.64 = (f32[2048]{0:T(1024)S(1)}, f32[2048]{0:T(1024)S(1)}, f32[2048]{0:T(1024)S(1)}, f32[2048]{0:T(1024)S(1)}, f32[2048]{0:T(1024)S(1)}, /*index=5*/f32[2048]{0:T(1024)S(1)}) fusion(f32[2048]{0:T(1024)S(1)} %bitcast.257, f32[1024]{0:T(1024)S(1)} %bitcast.269, f32[2048]{0:T(1024)S(1)} %bitcast.254, f32[1024]{0:T(1024)S(1)} %bitcast.272, ...), kind=kLoop, calls=%fused_computation.45.clone.1 | loop fusion | flops 85970944 | bytes 122880 | tf_op jit(solution)/shard_map/while/body/eval_jaxpr/reduce_sum | solution.py:28
  111.2 16.2 %fusion.64 = (f32[2048]{0:T(1024)S(1)}, f32[2048]{0:T(1024)S(1)}, f32[2048]{0:T(1024)S(1)}, f32[2048]{0:T(1024)S(1)}, f32[2048]{0:T(1024)S(1)}, /*index=5*/f32[2048]{0:T(1024)S(1)}) fusion(f32[2048]{0:T(1024)S(1)} %bitcast.257, f32[1024]{0:T(1024)S(1)} %bitcast.269, f32[2048]{0:T(1024)S(1)} %bitcast.254, f32[1024]{0:T(1024)S(1)} %bitcast.272, ...), kind=kLoop, calls=%fused_computation.45.clone.1 | loop fusion | flops 85970944 | bytes 122880 | tf_op jit(solution)/shard_map/while/body/eval_jaxpr/reduce_sum | solution.py:28
  127.7 16.2 %fusion.64 = (f32[2048]{0:T(1024)S(1)}, f32[2048]{0:T(1024)S(1)}, f32[2048]{0:T(1024)S(1)}, f32[2048]{0:T(1024)S(1)}, f32[2048]{0:T(1024)S(1)}, /*index=5*/f32[2048]{0:T(1024)S(1)}) fusion(f32[2048]{0:T(1024)S(1)} %bitcast.257, f32[1024]{0:T(1024)S(1)} %bitcast.269, f32[2048]{0:T(1024)S(1)} %bitcast.254, f32[1024]{0:T(1024)S(1)} %bitcast.272, ...), kind=kLoop, calls=%fused_computation.45.clone.1 | loop fusion | flops 85970944 | bytes 122880 | tf_op jit(solution)/shard_map/while/body/eval_jaxpr/reduce_sum | solution.py:28
  144.2 16.2 %fusion.64 = (f32[2048]{0:T(1024)S(1)}, f32[2048]{0:T(1024)S(1)}, f32[2048]{0:T(1024)S(1)}, f32[2048]{0:T(1024)S(1)}, f32[2048]{0:T(1024)S(1)}, /*index=5*/f32[2048]{0:T(1024)S(1)}) fusion(f32[2048]{0:T(1024)S(1)} %bitcast.257, f32[1024]{0:T(1024)S(1)} %bitcast.269, f32[2048]{0:T(1024)S(1)} %bitcast.254, f32[1024]{0:T(1024)S(1)} %bitcast.272, ...), kind=kLoop, calls=%fused_computation.45.clone.1 | loop fusion | flops 85970944 | bytes 122880 | tf_op jit(solution)/shard_map/while/body/eval_jaxpr/reduce_sum | solution.py:28
  160.6 16.2 %fusion.64 = (f32[2048]{0:T(1024)S(1)}, f32[2048]{0:T(1024)S(1)}, f32[2048]{0:T(1024)S(1)}, f32[2048]{0:T(1024)S(1)}, f32[2048]{0:T(1024)S(1)}, /*index=5*/f32[2048]{0:T(1024)S(1)}) fusion(f32[2048]{0:T(1024)S(1)} %bitcast.257, f32[1024]{0:T(1024)S(1)} %bitcast.269, f32[2048]{0:T(1024)S(1)} %bitcast.254, f32[1024]{0:T(1024)S(1)} %bitcast.272, ...), kind=kLoop, calls=%fused_computation.45.clone.1 | loop fusion | flops 85970944 | bytes 122880 | tf_op jit(solution)/shard_map/while/body/eval_jaxpr/reduce_sum | solution.py:28
  177.1 16.2 %fusion.64 = (f32[2048]{0:T(1024)S(1)}, f32[2048]{0:T(1024)S(1)}, f32[2048]{0:T(1024)S(1)}, f32[2048]{0:T(1024)S(1)}, f32[2048]{0:T(1024)S(1)}, /*index=5*/f32[2048]{0:T(1024)S(1)}) fusion(f32[2048]{0:T(1024)S(1)} %bitcast.257, f32[1024]{0:T(1024)S(1)} %bitcast.269, f32[2048]{0:T(1024)S(1)} %bitcast.254, f32[1024]{0:T(1024)S(1)} %bitcast.272, ...), kind=kLoop, calls=%fused_computation.45.clone.1 | loop fusion | flops 85970944 | bytes 122880 | tf_op jit(solution)/shard_map/while/body/eval_jaxpr/reduce_sum | solution.py:28
  193.5 16.2 %fusion.64 = (f32[2048]{0:T(1024)S(1)}, f32[2048]{0:T(1024)S(1)}, f32[2048]{0:T(1024)S(1)}, f32[2048]{0:T(1024)S(1)}, f32[2048]{0:T(1024)S(1)}, /*index=5*/f32[2048]{0:T(1024)S(1)}) fusion(f32[2048]{0:T(1024)S(1)} %bitcast.257, f32[1024]{0:T(1024)S(1)} %bitcast.269, f32[2048]{0:T(1024)S(1)} %bitcast.254, f32[1024]{0:T(1024)S(1)} %bitcast.272, ...), kind=kLoop, calls=%fused_computation.45.clone.1 | loop fusion | flops 85970944 | bytes 122880 | tf_op jit(solution)/shard_map/while/body/eval_jaxpr/reduce_sum | solution.py:28
  210.0 16.2 %fusion.64 = (f32[2048]{0:T(1024)S(1)}, f32[2048]{0:T(1024)S(1)}, f32[2048]{0:T(1024)S(1)}, f32[2048]{0:T(1024)S(1)}, f32[2048]{0:T(1024)S(1)}, /*index=5*/f32[2048]{0:T(1024)S(1)}) fusion(f32[2048]{0:T(1024)S(1)} %bitcast.257, f32[1024]{0:T(1024)S(1)} %bitcast.269, f32[2048]{0:T(1024)S(1)} %bitcast.254, f32[1024]{0:T(1024)S(1)} %bitcast.272, ...), kind=kLoop, calls=%fused_computation.45.clone.1 | loop fusion | flops 85970944 | bytes 122880 | tf_op jit(solution)/shard_map/while/body/eval_jaxpr/reduce_sum | solution.py:28
  226.4 16.2 %fusion.64 = (f32[2048]{0:T(1024)S(1)}, f32[2048]{0:T(1024)S(1)}, f32[2048]{0:T(1024)S(1)}, f32[2048]{0:T(1024)S(1)}, f32[2048]{0:T(1024)S(1)}, /*index=5*/f32[2048]{0:T(1024)S(1)}) fusion(f32[2048]{0:T(1024)S(1)} %bitcast.257, f32[1024]{0:T(1024)S(1)} %bitcast.269, f32[2048]{0:T(1024)S(1)} %bitcast.254, f32[1024]{0:T(1024)S(1)} %bitcast.272, ...), kind=kLoop, calls=%fused_computation.45.clone.1 | loop fusion | flops 85970944 | bytes 122880 | tf_op jit(solution)/shard_map/while/body/eval_jaxpr/reduce_sum | solution.py:28
  242.9 16.2 %fusion.64 = (f32[2048]{0:T(1024)S(1)}, f32[2048]{0:T(1024)S(1)}, f32[2048]{0:T(1024)S(1)}, f32[2048]{0:T(1024)S(1)}, f32[2048]{0:T(1024)S(1)}, /*index=5*/f32[2048]{0:T(1024)S(1)}) fusion(f32[2048]{0:T(1024)S(1)} %bitcast.257, f32[1024]{0:T(1024)S(1)} %bitcast.269, f32[2048]{0:T(1024)S(1)} %bitcast.254, f32[1024]{0:T(1024)S(1)} %bitcast.272, ...), kind=kLoop, calls=%fused_computation.45.clone.1 | loop fusion | flops 85970944 | bytes 122880 | tf_op jit(solution)/shard_map/while/body/eval_jaxpr/reduce_sum | solution.py:28
  259.3 16.2 %fusion.64 = (f32[2048]{0:T(1024)S(1)}, f32[2048]{0:T(1024)S(1)}, f32[2048]{0:T(1024)S(1)}, f32[2048]{0:T(1024)S(1)}, f32[2048]{0:T(1024)S(1)}, /*index=5*/f32[2048]{0:T(1024)S(1)}) fusion(f32[2048]{0:T(1024)S(1)} %bitcast.257, f32[1024]{0:T(1024)S(1)} %bitcast.269, f32[2048]{0:T(1024)S(1)} %bitcast.254, f32[1024]{0:T(1024)S(1)} %bitcast.272, ...), kind=kLoop, calls=%fused_computation.45.clone.1 | loop fusion | flops 85970944 | bytes 122880 | tf_op jit(solution)/shard_map/while/body/eval_jaxpr/reduce_sum | solution.py:28
  275.8 16.2 %fusion.64 = (f32[2048]{0:T(1024)S(1)}, f32[2048]{0:T(1024)S(1)}, f32[2048]{0:T(1024)S(1)}, f32[2048]{0:T(1024)S(1)}, f32[2048]{0:T(1024)S(1)}, /*index=5*/f32[2048]{0:T(1024)S(1)}) fusion(f32[2048]{0:T(1024)S(1)} %bitcast.257, f32[1024]{0:T(1024)S(1)} %bitcast.269, f32[2048]{0:T(1024)S(1)} %bitcast.254, f32[1024]{0:T(1024)S(1)} %bitcast.272, ...), kind=kLoop, calls=%fused_computation.45.clone.1 | loop fusion | flops 85970944 | bytes 122880 | tf_op jit(solution)/shard_map/while/body/eval_jaxpr/reduce_sum | solution.py:28
  292.2 16.2 %fusion.64 = (f32[2048]{0:T(1024)S(1)}, f32[2048]{0:T(1024)S(1)}, f32[2048]{0:T(1024)S(1)}, f32[2048]{0:T(1024)S(1)}, f32[2048]{0:T(1024)S(1)}, /*index=5*/f32[2048]{0:T(1024)S(1)}) fusion(f32[2048]{0:T(1024)S(1)} %bitcast.257, f32[1024]{0:T(1024)S(1)} %bitcast.269, f32[2048]{0:T(1024)S(1)} %bitcast.254, f32[1024]{0:T(1024)S(1)} %bitcast.272, ...), kind=kLoop, calls=%fused_computation.45.clone.1 | loop fusion | flops 85970944 | bytes 122880 | tf_op jit(solution)/shard_map/while/body/eval_jaxpr/reduce_sum | solution.py:28
  308.7 16.2 %fusion.64 = (f32[2048]{0:T(1024)S(1)}, f32[2048]{0:T(1024)S(1)}, f32[2048]{0:T(1024)S(1)}, f32[2048]{0:T(1024)S(1)}, f32[2048]{0:T(1024)S(1)}, /*index=5*/f32[2048]{0:T(1024)S(1)}) fusion(f32[2048]{0:T(1024)S(1)} %bitcast.257, f32[1024]{0:T(1024)S(1)} %bitcast.269, f32[2048]{0:T(1024)S(1)} %bitcast.254, f32[1024]{0:T(1024)S(1)} %bitcast.272, ...), kind=kLoop, calls=%fused_computation.45.clone.1 | loop fusion | flops 85970944 | bytes 122880 | tf_op jit(solution)/shard_map/while/body/eval_jaxpr/reduce_sum | solution.py:28
  325.1 16.2 %fusion.64 = (f32[2048]{0:T(1024)S(1)}, f32[2048]{0:T(1024)S(1)}, f32[2048]{0:T(1024)S(1)}, f32[2048]{0:T(1024)S(1)}, f32[2048]{0:T(1024)S(1)}, /*index=5*/f32[2048]{0:T(1024)S(1)}) fusion(f32[2048]{0:T(1024)S(1)} %bitcast.257, f32[1024]{0:T(1024)S(1)} %bitcast.269, f32[2048]{0:T(1024)S(1)} %bitcast.254, f32[1024]{0:T(1024)S(1)} %bitcast.272, ...), kind=kLoop, calls=%fused_computation.45.clone.1 | loop fusion | flops 85970944 | bytes 122880 | tf_op jit(solution)/shard_map/while/body/eval_jaxpr/reduce_sum | solution.py:28
  349.7 139.0 %all-reduce.3.cloned.1.call-done = f32[6,32768]{1,0:T(8,128)} async-done(((f32[6,32768]{1,0:T(8,128)}), f32[6,32768]{1,0:T(8,128)}) %all-reduce.3.cloned.1.call-update) | async-done | bytes 786448 | tf_op jit(solution)/shard_map/psum | solution.py:79
  498.1 64.6 %all-gather.3 = f32[128,6,256]{2,1,0:T(8,128)} all-gather(f32[1,6,256]{2,1,0:T(8,128)S(1)} %maximum_bitcast_fusion.1), channel_id=3, replica_groups=mesh['grp'=8,'dev'=16] {'grp','dev'}, dimensions={0}, use_global_device_ids=true | all-gather | bytes 792576 | tf_op jit(solution)/shard_map/all_gather | solution.py:76
  562.8 280.6 %while.21 = (s32[]{:T(128)}, f32[16,6,2048]{2,1,0:T(8,128)S(1)}, f32[3,1024]{1,0:T(4,128)S(1)}, f32[16,6,2048]{2,1,0:T(8,128)}, f32[3,1024]{1,0:T(4,128)S(1)}, /...) while((s32[]{:T(128)}, f32[16,6,2048]{2,1,0:T(8,128)S(1)}, ...), condition=%wide.region_21.22_spmd, body=%wide.region_14.21_spmd.sunk | while | flops 85970952 | bytes 499917 | solution.py:37
  564.0 16.2 %fusion.66 = (f32[2048]{0:T(1024)S(1)}, f32[2048]{0:T(1024)S(1)}, f32[2048]{0:T(1024)S(1)}, f32[2048]{0:T(1024)S(1)}, f32[2048]{0:T(1024)S(1)}, /*index=5*/f32[2048]{0:T(1024)S(1)}) fusion(f32[2048]{0:T(1024)S(1)} %bitcast.263, f32[1024]{0:T(1024)S(1)} %bitcast.275, f32[2048]{0:T(1024)S(1)} %bitcast.260, f32[1024]{0:T(1024)S(1)} %bitcast.278, ...), kind=kLoop, calls=%fused_computation.85.clone.1 | loop fusion | flops 85970944 | bytes 122880 | tf_op jit(solution)/shard_map/while/body/eval_jaxpr/reduce_sum | solution.py:28
  581.5 16.2 %fusion.66 = (f32[2048]{0:T(1024)S(1)}, f32[2048]{0:T(1024)S(1)}, f32[2048]{0:T(1024)S(1)}, f32[2048]{0:T(1024)S(1)}, f32[2048]{0:T(1024)S(1)}, /*index=5*/f32[2048]{0:T(1024)S(1)}) fusion(f32[2048]{0:T(1024)S(1)} %bitcast.263, f32[1024]{0:T(1024)S(1)} %bitcast.275, f32[2048]{0:T(1024)S(1)} %bitcast.260, f32[1024]{0:T(1024)S(1)} %bitcast.278, ...), kind=kLoop, calls=%fused_computation.85.clone.1 | loop fusion | flops 85970944 | bytes 122880 | tf_op jit(solution)/shard_map/while/body/eval_jaxpr/reduce_sum | solution.py:28
  599.2 16.2 %fusion.66 = (f32[2048]{0:T(1024)S(1)}, f32[2048]{0:T(1024)S(1)}, f32[2048]{0:T(1024)S(1)}, f32[2048]{0:T(1024)S(1)}, f32[2048]{0:T(1024)S(1)}, /*index=5*/f32[2048]{0:T(1024)S(1)}) fusion(f32[2048]{0:T(1024)S(1)} %bitcast.263, f32[1024]{0:T(1024)S(1)} %bitcast.275, f32[2048]{0:T(1024)S(1)} %bitcast.260, f32[1024]{0:T(1024)S(1)} %bitcast.278, ...), kind=kLoop, calls=%fused_computation.85.clone.1 | loop fusion | flops 85970944 | bytes 122880 | tf_op jit(solution)/shard_map/while/body/eval_jaxpr/reduce_sum | solution.py:28
  616.7 16.2 %fusion.66 = (f32[2048]{0:T(1024)S(1)}, f32[2048]{0:T(1024)S(1)}, f32[2048]{0:T(1024)S(1)}, f32[2048]{0:T(1024)S(1)}, f32[2048]{0:T(1024)S(1)}, /*index=5*/f32[2048]{0:T(1024)S(1)}) fusion(f32[2048]{0:T(1024)S(1)} %bitcast.263, f32[1024]{0:T(1024)S(1)} %bitcast.275, f32[2048]{0:T(1024)S(1)} %bitcast.260, f32[1024]{0:T(1024)S(1)} %bitcast.278, ...), kind=kLoop, calls=%fused_computation.85.clone.1 | loop fusion | flops 85970944 | bytes 122880 | tf_op jit(solution)/shard_map/while/body/eval_jaxpr/reduce_sum | solution.py:28
  634.2 16.2 %fusion.66 = (f32[2048]{0:T(1024)S(1)}, f32[2048]{0:T(1024)S(1)}, f32[2048]{0:T(1024)S(1)}, f32[2048]{0:T(1024)S(1)}, f32[2048]{0:T(1024)S(1)}, /*index=5*/f32[2048]{0:T(1024)S(1)}) fusion(f32[2048]{0:T(1024)S(1)} %bitcast.263, f32[1024]{0:T(1024)S(1)} %bitcast.275, f32[2048]{0:T(1024)S(1)} %bitcast.260, f32[1024]{0:T(1024)S(1)} %bitcast.278, ...), kind=kLoop, calls=%fused_computation.85.clone.1 | loop fusion | flops 85970944 | bytes 122880 | tf_op jit(solution)/shard_map/while/body/eval_jaxpr/reduce_sum | solution.py:28
  651.8 16.2 %fusion.66 = (f32[2048]{0:T(1024)S(1)}, f32[2048]{0:T(1024)S(1)}, f32[2048]{0:T(1024)S(1)}, f32[2048]{0:T(1024)S(1)}, f32[2048]{0:T(1024)S(1)}, /*index=5*/f32[2048]{0:T(1024)S(1)}) fusion(f32[2048]{0:T(1024)S(1)} %bitcast.263, f32[1024]{0:T(1024)S(1)} %bitcast.275, f32[2048]{0:T(1024)S(1)} %bitcast.260, f32[1024]{0:T(1024)S(1)} %bitcast.278, ...), kind=kLoop, calls=%fused_computation.85.clone.1 | loop fusion | flops 85970944 | bytes 122880 | tf_op jit(solution)/shard_map/while/body/eval_jaxpr/reduce_sum | solution.py:28
  669.3 16.2 %fusion.66 = (f32[2048]{0:T(1024)S(1)}, f32[2048]{0:T(1024)S(1)}, f32[2048]{0:T(1024)S(1)}, f32[2048]{0:T(1024)S(1)}, f32[2048]{0:T(1024)S(1)}, /*index=5*/f32[2048]{0:T(1024)S(1)}) fusion(f32[2048]{0:T(1024)S(1)} %bitcast.263, f32[1024]{0:T(1024)S(1)} %bitcast.275, f32[2048]{0:T(1024)S(1)} %bitcast.260, f32[1024]{0:T(1024)S(1)} %bitcast.278, ...), kind=kLoop, calls=%fused_computation.85.clone.1 | loop fusion | flops 85970944 | bytes 122880 | tf_op jit(solution)/shard_map/while/body/eval_jaxpr/reduce_sum | solution.py:28
  739.4 16.2 %fusion.66 = (f32[2048]{0:T(1024)S(1)}, f32[2048]{0:T(1024)S(1)}, f32[2048]{0:T(1024)S(1)}, f32[2048]{0:T(1024)S(1)}, f32[2048]{0:T(1024)S(1)}, /*index=5*/f32[2048]{0:T(1024)S(1)}) fusion(f32[2048]{0:T(1024)S(1)} %bitcast.263, f32[1024]{0:T(1024)S(1)} %bitcast.275, f32[2048]{0:T(1024)S(1)} %bitcast.260, f32[1024]{0:T(1024)S(1)} %bitcast.278, ...), kind=kLoop, calls=%fused_computation.85.clone.1 | loop fusion | flops 85970944 | bytes 122880 | tf_op jit(solution)/shard_map/while/body/eval_jaxpr/reduce_sum | solution.py:28
  757.0 16.2 %fusion.66 = (f32[2048]{0:T(1024)S(1)}, f32[2048]{0:T(1024)S(1)}, f32[2048]{0:T(1024)S(1)}, f32[2048]{0:T(1024)S(1)}, f32[2048]{0:T(1024)S(1)}, /*index=5*/f32[2048]{0:T(1024)S(1)}) fusion(f32[2048]{0:T(1024)S(1)} %bitcast.263, f32[1024]{0:T(1024)S(1)} %bitcast.275, f32[2048]{0:T(1024)S(1)} %bitcast.260, f32[1024]{0:T(1024)S(1)} %bitcast.278, ...), kind=kLoop, calls=%fused_computation.85.clone.1 | loop fusion | flops 85970944 | bytes 122880 | tf_op jit(solution)/shard_map/while/body/eval_jaxpr/reduce_sum | solution.py:28
  774.5 16.2 %fusion.66 = (f32[2048]{0:T(1024)S(1)}, f32[2048]{0:T(1024)S(1)}, f32[2048]{0:T(1024)S(1)}, f32[2048]{0:T(1024)S(1)}, f32[2048]{0:T(1024)S(1)}, /*index=5*/f32[2048]{0:T(1024)S(1)}) fusion(f32[2048]{0:T(1024)S(1)} %bitcast.263, f32[1024]{0:T(1024)S(1)} %bitcast.275, f32[2048]{0:T(1024)S(1)} %bitcast.260, f32[1024]{0:T(1024)S(1)} %bitcast.278, ...), kind=kLoop, calls=%fused_computation.85.clone.1 | loop fusion | flops 85970944 | bytes 122880 | tf_op jit(solution)/shard_map/while/body/eval_jaxpr/reduce_sum | solution.py:28
  849.1 141.9 %all-reduce.5.cloned.1.call-done = f32[6,32768]{1,0:T(8,128)} async-done(((f32[6,32768]{1,0:T(8,128)}), f32[6,32768]{1,0:T(8,128)}) %all-reduce.5.cloned.1.call-update) | async-done | bytes 786448 | tf_op jit(solution)/shard_map/psum | solution.py:79
  (223 shorter events, 160.9 us)
Async XLA Ops:
  7.2 481.4 %all-reduce.3.cloned.1.call-start = ((), (), s32[]{:S(2)}) async-start(), calls=%async_computation | async-start | bytes 2097152 | tf_op jit(solution)/shard_map/psum | solution.py:79
  341.5 1.0 copy-start.1
  341.5 1.1 copy-start.2
  341.5 1.3 copy-start.3
  341.5 1.6 copy-start.4
  342.5 0.8 copy-start.5
  342.6 648.4 %all-reduce.5.cloned.1.call-start = ((), (), s32[]{:S(2)}) async-start(), calls=%async_computation.1 | async-start | bytes 2097152 | tf_op jit(solution)/shard_map/psum | solution.py:79
  843.4 1.0 copy-start
Sparse Core Ops, SparseCore 0:
  342.7 145.8 all-reduce.2
  844.6 146.3 all-reduce.4
where the time goes:
time: 1010 us
  other arithmetic  525 us (52%)
  waiting for transfers between devices  281 us (28%)
  blocking collectives  129 us (13%)
  local copies, waits for them, and re-layouts  57.6 us (6%)
  between operations  14.4 us (1%)
    reduce_sum x32, other arithmetic, pair_block(): jnp.sum(weight * (drift_z - along * gap_z), axis=1)  519 us
    psum x2, waiting for transfers between devices, shards(): totals = lax.psum(terms, ('grp', 'dev'))  281 us
    all_gather x2, blocking collectives, shards(): gathered = lax.all_gather(targets[None], ('grp', 'dev'), axis=0, tiled=True)  129 us
  transfers between devices with their start and end apart: 2, of which 2 were waited for; matrix products, arithmetic and copies ran while one was open for 1% of the time, Pallas kernels for 0%

commit v1 on v0

--- a/solution.py
+++ b/solution.py
@@ -73,7 +73,11 @@
         targets = jnp.concatenate([pred_pos[:, rows], pred_vel[:, rows]], axis=0)
         step_counts = counts[step]
         own_count = step_counts[my_rank]
-        gathered = lax.all_gather(targets[None], ("grp", "dev"), axis=0, tiled=True)
+        x = targets[None]
+        count = lax.axis_size(("grp", "dev"))
+        pieces = jnp.stack([x for _ in range(count)])
+        pieces = lax.all_to_all(pieces, ("grp", "dev"), split_axis=0, concat_axis=0)
+        gathered = jnp.concatenate(pieces, axis=0)
         flat = gathered.transpose(1, 0, 2).reshape(6, devices_all * slot_cap)
         terms = block_terms(flat, pred_pos, pred_vel, mass, soft_sq)
         totals = lax.psum(terms, ("grp", "dev"))

time: 1010 us -> 955 us (0.946)
  blocking collectives: 129 us -> 0 us
  local copies, waits for them, and re-layouts: 57.6 us -> 86.1 us
  waiting for transfers between devices: 281 us -> 307 us
  starting transfers between devices: 0.08 us -> 18.4 us
    all_gather x2 -> x0, blocking collectives: 129 us -> none  [shards(): gathered = lax.all_gather(targets[None], ('grp', 'dev'), axis=0, tiled=True)]
    all_to_all x0 -> x2, waiting for transfers between devices: none -> 24.6 us  [shards(): pieces = lax.all_to_all(pieces, ('grp', 'dev'), split_axis=0, concat_axis=0)]
    all_to_all x0 -> x2, starting transfers between devices: none -> 18.3 us  [shards(): pieces = lax.all_to_all(pieces, ('grp', 'dev'), split_axis=0, concat_axis=0)]
    slice x64, local copies, waits for them, and re-layouts: 20.1 us -> 37.6 us  [pair_block(): drift_x = src_vel[0][None, :] - targets[3][:, None]]
  transfers between devices with their start and end apart: 2 -> 4, of which waited for: 2 -> 4; matrix products, arithmetic and copies ran while one was open for 1% -> 1% of each run, Pallas kernels for 0% -> 0%
where the time goes in v1:
time: 955 us; the launch traced here: 952 us
  other arithmetic  525 us (55%)
  waiting for transfers between devices  307 us (32%)
  local copies, waits for them, and re-layouts  86.1 us (9%)
  starting transfers between devices  18.4 us (2%)
  between operations  14.4 us (2%)
    reduce_sum x32, other arithmetic, pair_block(): jnp.sum(weight * (drift_z - along * gap_z), axis=1)  519 us
    psum x2, waiting for transfers between devices, shards(): totals = lax.psum(terms, ('grp', 'dev'))  282 us
    slice x64, local copies, waits for them, and re-layouts, pair_block(): drift_x = src_vel[0][None, :] - targets[3][:, None]  37.6 us
    all_to_all x2, waiting for transfers between devices, shards(): pieces = lax.all_to_all(pieces, ('grp', 'dev'), split_axis=0, concat_axis=0)  24.6 us
  transfers between devices with their start and end apart: 4, of which 4 were waited for; matrix products, arithmetic and copies ran while one was open for 1% of the time, Pallas kernels for 0%

profile of v1, /device:TPU:1, one launch (start us, length us, event | category | flops | bytes accessed | tf_op | source)
XLA Modules:
  0.0 952.1 jit_solution(11936273569696493552)
XLA Ops:
  47.3 280.6 %while.20 = (s32[]{:T(128)}, f32[16,6,2048]{2,1,0:T(8,128)S(1)}, f32[3,1024]{1,0:T(4,128)S(1)}, f32[16,6,2048]{2,1,0:T(8,128)}, f32[3,1024]{1,0:T(4,128)S(1)}, /...) while((s32[]{:T(128)}, f32[16,6,2048]{2,1,0:T(8,128)S(1)}, f32[3,1024]{1,0:T(4,128)S(1)}, ...), condition=%wide.region_7.8_spmd, body=%wide.region_0.7_spmd.sunk | while | flops 85970952 | bytes 499917 | solution.py:37
  48.5 16.2 %fusion.64 = (f32[2048]{0:T(1024)S(1)}, f32[2048]{0:T(1024)S(1)}, f32[2048]{0:T(1024)S(1)}, f32[2048]{0:T(1024)S(1)}, f32[2048]{0:T(1024)S(1)}, /*index=5*/f32[2048]{0:T(1024)S(1)}) fusion(f32[2048]{0:T(1024)S(1)} %bitcast.261, f32[1024]{0:T(1024)S(1)} %bitcast.273, f32[2048]{0:T(1024)S(1)} %bitcast.258, f32[1024]{0:T(1024)S(1)} %bitcast.276, ...), kind=kLoop, calls=%fused_computation.45.clone.1 | loop fusion | flops 85970944 | bytes 122880 | tf_op jit(solution)/shard_map/while/body/eval_jaxpr/reduce_sum | solution.py:28
  66.0 16.2 %fusion.64 = (f32[2048]{0:T(1024)S(1)}, f32[2048]{0:T(1024)S(1)}, f32[2048]{0:T(1024)S(1)}, f32[2048]{0:T(1024)S(1)}, f32[2048]{0:T(1024)S(1)}, /*index=5*/f32[2048]{0:T(1024)S(1)}) fusion(f32[2048]{0:T(1024)S(1)} %bitcast.261, f32[1024]{0:T(1024)S(1)} %bitcast.273, f32[2048]{0:T(1024)S(1)} %bitcast.258, f32[1024]{0:T(1024)S(1)} %bitcast.276, ...), kind=kLoop, calls=%fused_computation.45.clone.1 | loop fusion | flops 85970944 | bytes 122880 | tf_op jit(solution)/shard_map/while/body/eval_jaxpr/reduce_sum | solution.py:28
  83.7 16.2 %fusion.64 = (f32[2048]{0:T(1024)S(1)}, f32[2048]{0:T(1024)S(1)}, f32[2048]{0:T(1024)S(1)}, f32[2048]{0:T(1024)S(1)}, f32[2048]{0:T(1024)S(1)}, /*index=5*/f32[2048]{0:T(1024)S(1)}) fusion(f32[2048]{0:T(1024)S(1)} %bitcast.261, f32[1024]{0:T(1024)S(1)} %bitcast.273, f32[2048]{0:T(1024)S(1)} %bitcast.258, f32[1024]{0:T(1024)S(1)} %bitcast.276, ...), kind=kLoop, calls=%fused_computation.45.clone.1 | loop fusion | flops 85970944 | bytes 122880 | tf_op jit(solution)/shard_map/while/body/eval_jaxpr/reduce_sum | solution.py:28
  101.2 16.2 %fusion.64 = (f32[2048]{0:T(1024)S(1)}, f32[2048]{0:T(1024)S(1)}, f32[2048]{0:T(1024)S(1)}, f32[2048]{0:T(1024)S(1)}, f32[2048]{0:T(1024)S(1)}, /*index=5*/f32[2048]{0:T(1024)S(1)}) fusion(f32[2048]{0:T(1024)S(1)} %bitcast.261, f32[1024]{0:T(1024)S(1)} %bitcast.273, f32[2048]{0:T(1024)S(1)} %bitcast.258, f32[1024]{0:T(1024)S(1)} %bitcast.276, ...), kind=kLoop, calls=%fused_computation.45.clone.1 | loop fusion | flops 85970944 | bytes 122880 | tf_op jit(solution)/shard_map/while/body/eval_jaxpr/reduce_sum | solution.py:28
  136.3 16.2 %fusion.64 = (f32[2048]{0:T(1024)S(1)}, f32[2048]{0:T(1024)S(1)}, f32[2048]{0:T(1024)S(1)}, f32[2048]{0:T(1024)S(1)}, f32[2048]{0:T(1024)S(1)}, /*index=5*/f32[2048]{0:T(1024)S(1)}) fusion(f32[2048]{0:T(1024)S(1)} %bitcast.261, f32[1024]{0:T(1024)S(1)} %bitcast.273, f32[2048]{0:T(1024)S(1)} %bitcast.258, f32[1024]{0:T(1024)S(1)} %bitcast.276, ...), kind=kLoop, calls=%fused_computation.45.clone.1 | loop fusion | flops 85970944 | bytes 122880 | tf_op jit(solution)/shard_map/while/body/eval_jaxpr/reduce_sum | solution.py:28
  171.4 16.2 %fusion.64 = (f32[2048]{0:T(1024)S(1)}, f32[2048]{0:T(1024)S(1)}, f32[2048]{0:T(1024)S(1)}, f32[2048]{0:T(1024)S(1)}, f32[2048]{0:T(1024)S(1)}, /*index=5*/f32[2048]{0:T(1024)S(1)}) fusion(f32[2048]{0:T(1024)S(1)} %bitcast.261, f32[1024]{0:T(1024)S(1)} %bitcast.273, f32[2048]{0:T(1024)S(1)} %bitcast.258, f32[1024]{0:T(1024)S(1)} %bitcast.276, ...), kind=kLoop, calls=%fused_computation.45.clone.1 | loop fusion | flops 85970944 | bytes 122880 | tf_op jit(solution)/shard_map/while/body/eval_jaxpr/reduce_sum | solution.py:28
  188.9 16.2 %fusion.64 = (f32[2048]{0:T(1024)S(1)}, f32[2048]{0:T(1024)S(1)}, f32[2048]{0:T(1024)S(1)}, f32[2048]{0:T(1024)S(1)}, f32[2048]{0:T(1024)S(1)}, /*index=5*/f32[2048]{0:T(1024)S(1)}) fusion(f32[2048]{0:T(1024)S(1)} %bitcast.261, f32[1024]{0:T(1024)S(1)} %bitcast.273, f32[2048]{0:T(1024)S(1)} %bitcast.258, f32[1024]{0:T(1024)S(1)} %bitcast.276, ...), kind=kLoop, calls=%fused_computation.45.clone.1 | loop fusion | flops 85970944 | bytes 122880 | tf_op jit(solution)/shard_map/while/body/eval_jaxpr/reduce_sum | solution.py:28
  206.4 16.2 %fusion.64 = (f32[2048]{0:T(1024)S(1)}, f32[2048]{0:T(1024)S(1)}, f32[2048]{0:T(1024)S(1)}, f32[2048]{0:T(1024)S(1)}, f32[2048]{0:T(1024)S(1)}, /*index=5*/f32[2048]{0:T(1024)S(1)}) fusion(f32[2048]{0:T(1024)S(1)} %bitcast.261, f32[1024]{0:T(1024)S(1)} %bitcast.273, f32[2048]{0:T(1024)S(1)} %bitcast.258, f32[1024]{0:T(1024)S(1)} %bitcast.276, ...), kind=kLoop, calls=%fused_computation.45.clone.1 | loop fusion | flops 85970944 | bytes 122880 | tf_op jit(solution)/shard_map/while/body/eval_jaxpr/reduce_sum | solution.py:28
  259.0 16.2 %fusion.64 = (f32[2048]{0:T(1024)S(1)}, f32[2048]{0:T(1024)S(1)}, f32[2048]{0:T(1024)S(1)}, f32[2048]{0:T(1024)S(1)}, f32[2048]{0:T(1024)S(1)}, /*index=5*/f32[2048]{0:T(1024)S(1)}) fusion(f32[2048]{0:T(1024)S(1)} %bitcast.261, f32[1024]{0:T(1024)S(1)} %bitcast.273, f32[2048]{0:T(1024)S(1)} %bitcast.258, f32[1024]{0:T(1024)S(1)} %bitcast.276, ...), kind=kLoop, calls=%fused_computation.45.clone.1 | loop fusion | flops 85970944 | bytes 122880 | tf_op jit(solution)/shard_map/while/body/eval_jaxpr/reduce_sum | solution.py:28
  276.5 16.2 %fusion.64 = (f32[2048]{0:T(1024)S(1)}, f32[2048]{0:T(1024)S(1)}, f32[2048]{0:T(1024)S(1)}, f32[2048]{0:T(1024)S(1)}, f32[2048]{0:T(1024)S(1)}, /*index=5*/f32[2048]{0:T(1024)S(1)}) fusion(f32[2048]{0:T(1024)S(1)} %bitcast.261, f32[1024]{0:T(1024)S(1)} %bitcast.273, f32[2048]{0:T(1024)S(1)} %bitcast.258, f32[1024]{0:T(1024)S(1)} %bitcast.276, ...), kind=kLoop, calls=%fused_computation.45.clone.1 | loop fusion | flops 85970944 | bytes 122880 | tf_op jit(solution)/shard_map/while/body/eval_jaxpr/reduce_sum | solution.py:28
  294.1 16.2 %fusion.64 = (f32[2048]{0:T(1024)S(1)}, f32[2048]{0:T(1024)S(1)}, f32[2048]{0:T(1024)S(1)}, f32[2048]{0:T(1024)S(1)}, f32[2048]{0:T(1024)S(1)}, /*index=5*/f32[2048]{0:T(1024)S(1)}) fusion(f32[2048]{0:T(1024)S(1)} %bitcast.261, f32[1024]{0:T(1024)S(1)} %bitcast.273, f32[2048]{0:T(1024)S(1)} %bitcast.258, f32[1024]{0:T(1024)S(1)} %bitcast.276, ...), kind=kLoop, calls=%fused_computation.45.clone.1 | loop fusion | flops 85970944 | bytes 122880 | tf_op jit(solution)/shard_map/while/body/eval_jaxpr/reduce_sum | solution.py:28
  311.6 16.2 %fusion.64 = (f32[2048]{0:T(1024)S(1)}, f32[2048]{0:T(1024)S(1)}, f32[2048]{0:T(1024)S(1)}, f32[2048]{0:T(1024)S(1)}, f32[2048]{0:T(1024)S(1)}, /*index=5*/f32[2048]{0:T(1024)S(1)}) fusion(f32[2048]{0:T(1024)S(1)} %bitcast.261, f32[1024]{0:T(1024)S(1)} %bitcast.273, f32[2048]{0:T(1024)S(1)} %bitcast.258, f32[1024]{0:T(1024)S(1)} %bitcast.276, ...), kind=kLoop, calls=%fused_computation.45.clone.1 | loop fusion | flops 85970944 | bytes 122880 | tf_op jit(solution)/shard_map/while/body/eval_jaxpr/reduce_sum | solution.py:28
  329.0 143.4 %all-reduce.3.cloned.1.call-done = f32[6,32768]{1,0:T(8,128)} async-done(((f32[6,32768]{1,0:T(8,128)}), f32[6,32768]{1,0:T(8,128)}) %all-reduce.3.cloned.1.call-update) | async-done | bytes 786448 | tf_op jit(solution)/shard_map/psum | solution.py:83
  510.0 280.8 %while.21 = (s32[]{:T(128)}, f32[16,6,2048]{2,1,0:T(8,128)S(1)}, f32[3,1024]{1,0:T(4,128)S(1)}, f32[16,6,2048]{2,1,0:T(8,128)}, f32[3,1024]{1,0:T(4,128)S(1)}, /...) while((s32[]{:T(128)}, f32[16,6,2048]{2,1,0:T(8,128)S(1)}, ...), condition=%wide.region_21.22_spmd, body=%wide.region_14.21_spmd.sunk | while | flops 85970952 | bytes 499917 | solution.py:37
  511.2 16.2 %fusion.66 = (f32[2048]{0:T(1024)S(1)}, f32[2048]{0:T(1024)S(1)}, f32[2048]{0:T(1024)S(1)}, f32[2048]{0:T(1024)S(1)}, f32[2048]{0:T(1024)S(1)}, /*index=5*/f32[2048]{0:T(1024)S(1)}) fusion(f32[2048]{0:T(1024)S(1)} %bitcast.267, f32[1024]{0:T(1024)S(1)} %bitcast.279, f32[2048]{0:T(1024)S(1)} %bitcast.264, f32[1024]{0:T(1024)S(1)} %bitcast.282, ...), kind=kLoop, calls=%fused_computation.85.clone.1 | loop fusion | flops 85970944 | bytes 122880 | tf_op jit(solution)/shard_map/while/body/eval_jaxpr/reduce_sum | solution.py:28
  528.7 16.2 %fusion.66 = (f32[2048]{0:T(1024)S(1)}, f32[2048]{0:T(1024)S(1)}, f32[2048]{0:T(1024)S(1)}, f32[2048]{0:T(1024)S(1)}, f32[2048]{0:T(1024)S(1)}, /*index=5*/f32[2048]{0:T(1024)S(1)}) fusion(f32[2048]{0:T(1024)S(1)} %bitcast.267, f32[1024]{0:T(1024)S(1)} %bitcast.279, f32[2048]{0:T(1024)S(1)} %bitcast.264, f32[1024]{0:T(1024)S(1)} %bitcast.282, ...), kind=kLoop, calls=%fused_computation.85.clone.1 | loop fusion | flops 85970944 | bytes 122880 | tf_op jit(solution)/shard_map/while/body/eval_jaxpr/reduce_sum | solution.py:28
  546.4 16.2 %fusion.66 = (f32[2048]{0:T(1024)S(1)}, f32[2048]{0:T(1024)S(1)}, f32[2048]{0:T(1024)S(1)}, f32[2048]{0:T(1024)S(1)}, f32[2048]{0:T(1024)S(1)}, /*index=5*/f32[2048]{0:T(1024)S(1)}) fusion(f32[2048]{0:T(1024)S(1)} %bitcast.267, f32[1024]{0:T(1024)S(1)} %bitcast.279, f32[2048]{0:T(1024)S(1)} %bitcast.264, f32[1024]{0:T(1024)S(1)} %bitcast.282, ...), kind=kLoop, calls=%fused_computation.85.clone.1 | loop fusion | flops 85970944 | bytes 122880 | tf_op jit(solution)/shard_map/while/body/eval_jaxpr/reduce_sum | solution.py:28
  563.9 16.2 %fusion.66 = (f32[2048]{0:T(1024)S(1)}, f32[2048]{0:T(1024)S(1)}, f32[2048]{0:T(1024)S(1)}, f32[2048]{0:T(1024)S(1)}, f32[2048]{0:T(1024)S(1)}, /*index=5*/f32[2048]{0:T(1024)S(1)}) fusion(f32[2048]{0:T(1024)S(1)} %bitcast.267, f32[1024]{0:T(1024)S(1)} %bitcast.279, f32[2048]{0:T(1024)S(1)} %bitcast.264, f32[1024]{0:T(1024)S(1)} %bitcast.282, ...), kind=kLoop, calls=%fused_computation.85.clone.1 | loop fusion | flops 85970944 | bytes 122880 | tf_op jit(solution)/shard_map/while/body/eval_jaxpr/reduce_sum | solution.py:28
  581.4 16.2 %fusion.66 = (f32[2048]{0:T(1024)S(1)}, f32[2048]{0:T(1024)S(1)}, f32[2048]{0:T(1024)S(1)}, f32[2048]{0:T(1024)S(1)}, f32[2048]{0:T(1024)S(1)}, /*index=5*/f32[2048]{0:T(1024)S(1)}) fusion(f32[2048]{0:T(1024)S(1)} %bitcast.267, f32[1024]{0:T(1024)S(1)} %bitcast.279, f32[2048]{0:T(1024)S(1)} %bitcast.264, f32[1024]{0:T(1024)S(1)} %bitcast.282, ...), kind=kLoop, calls=%fused_computation.85.clone.1 | loop fusion | flops 85970944 | bytes 122880 | tf_op jit(solution)/shard_map/while/body/eval_jaxpr/reduce_sum | solution.py:28
  599.0 16.2 %fusion.66 = (f32[2048]{0:T(1024)S(1)}, f32[2048]{0:T(1024)S(1)}, f32[2048]{0:T(1024)S(1)}, f32[2048]{0:T(1024)S(1)}, f32[2048]{0:T(1024)S(1)}, /*index=5*/f32[2048]{0:T(1024)S(1)}) fusion(f32[2048]{0:T(1024)S(1)} %bitcast.267, f32[1024]{0:T(1024)S(1)} %bitcast.279, f32[2048]{0:T(1024)S(1)} %bitcast.264, f32[1024]{0:T(1024)S(1)} %bitcast.282, ...), kind=kLoop, calls=%fused_computation.85.clone.1 | loop fusion | flops 85970944 | bytes 122880 | tf_op jit(solution)/shard_map/while/body/eval_jaxpr/reduce_sum | solution.py:28
  616.5 16.2 %fusion.66 = (f32[2048]{0:T(1024)S(1)}, f32[2048]{0:T(1024)S(1)}, f32[2048]{0:T(1024)S(1)}, f32[2048]{0:T(1024)S(1)}, f32[2048]{0:T(1024)S(1)}, /*index=5*/f32[2048]{0:T(1024)S(1)}) fusion(f32[2048]{0:T(1024)S(1)} %bitcast.267, f32[1024]{0:T(1024)S(1)} %bitcast.279, f32[2048]{0:T(1024)S(1)} %bitcast.264, f32[1024]{0:T(1024)S(1)} %bitcast.282, ...), kind=kLoop, calls=%fused_computation.85.clone.1 | loop fusion | flops 85970944 | bytes 122880 | tf_op jit(solution)/shard_map/while/body/eval_jaxpr/reduce_sum | solution.py:28
  634.1 16.2 %fusion.66 = (f32[2048]{0:T(1024)S(1)}, f32[2048]{0:T(1024)S(1)}, f32[2048]{0:T(1024)S(1)}, f32[2048]{0:T(1024)S(1)}, f32[2048]{0:T(1024)S(1)}, /*index=5*/f32[2048]{0:T(1024)S(1)}) fusion(f32[2048]{0:T(1024)S(1)} %bitcast.267, f32[1024]{0:T(1024)S(1)} %bitcast.279, f32[2048]{0:T(1024)S(1)} %bitcast.264, f32[1024]{0:T(1024)S(1)} %bitcast.282, ...), kind=kLoop, calls=%fused_computation.85.clone.1 | loop fusion | flops 85970944 | bytes 122880 | tf_op jit(solution)/shard_map/while/body/eval_jaxpr/reduce_sum | solution.py:28
  651.6 16.2 %fusion.66 = (f32[2048]{0:T(1024)S(1)}, f32[2048]{0:T(1024)S(1)}, f32[2048]{0:T(1024)S(1)}, f32[2048]{0:T(1024)S(1)}, f32[2048]{0:T(1024)S(1)}, /*index=5*/f32[2048]{0:T(1024)S(1)}) fusion(f32[2048]{0:T(1024)S(1)} %bitcast.267, f32[1024]{0:T(1024)S(1)} %bitcast.279, f32[2048]{0:T(1024)S(1)} %bitcast.264, f32[1024]{0:T(1024)S(1)} %bitcast.282, ...), kind=kLoop, calls=%fused_computation.85.clone.1 | loop fusion | flops 85970944 | bytes 122880 | tf_op jit(solution)/shard_map/while/body/eval_jaxpr/reduce_sum | solution.py:28
  669.1 16.2 %fusion.66 = (f32[2048]{0:T(1024)S(1)}, f32[2048]{0:T(1024)S(1)}, f32[2048]{0:T(1024)S(1)}, f32[2048]{0:T(1024)S(1)}, f32[2048]{0:T(1024)S(1)}, /*index=5*/f32[2048]{0:T(1024)S(1)}) fusion(f32[2048]{0:T(1024)S(1)} %bitcast.267, f32[1024]{0:T(1024)S(1)} %bitcast.279, f32[2048]{0:T(1024)S(1)} %bitcast.264, f32[1024]{0:T(1024)S(1)} %bitcast.282, ...), kind=kLoop, calls=%fused_computation.85.clone.1 | loop fusion | flops 85970944 | bytes 122880 | tf_op jit(solution)/shard_map/while/body/eval_jaxpr/reduce_sum | solution.py:28
  686.7 16.2 %fusion.66 = (f32[2048]{0:T(1024)S(1)}, f32[2048]{0:T(1024)S(1)}, f32[2048]{0:T(1024)S(1)}, f32[2048]{0:T(1024)S(1)}, f32[2048]{0:T(1024)S(1)}, /*index=5*/f32[2048]{0:T(1024)S(1)}) fusion(f32[2048]{0:T(1024)S(1)} %bitcast.267, f32[1024]{0:T(1024)S(1)} %bitcast.279, f32[2048]{0:T(1024)S(1)} %bitcast.264, f32[1024]{0:T(1024)S(1)} %bitcast.282, ...), kind=kLoop, calls=%fused_computation.85.clone.1 | loop fusion | flops 85970944 | bytes 122880 | tf_op jit(solution)/shard_map/while/body/eval_jaxpr/reduce_sum | solution.py:28
  704.2 16.2 %fusion.66 = (f32[2048]{0:T(1024)S(1)}, f32[2048]{0:T(1024)S(1)}, f32[2048]{0:T(1024)S(1)}, f32[2048]{0:T(1024)S(1)}, f32[2048]{0:T(1024)S(1)}, /*index=5*/f32[2048]{0:T(1024)S(1)}) fusion(f32[2048]{0:T(1024)S(1)} %bitcast.267, f32[1024]{0:T(1024)S(1)} %bitcast.279, f32[2048]{0:T(1024)S(1)} %bitcast.264, f32[1024]{0:T(1024)S(1)} %bitcast.282, ...), kind=kLoop, calls=%fused_computation.85.clone.1 | loop fusion | flops 85970944 | bytes 122880 | tf_op jit(solution)/shard_map/while/body/eval_jaxpr/reduce_sum | solution.py:28
  721.8 16.2 %fusion.66 = (f32[2048]{0:T(1024)S(1)}, f32[2048]{0:T(1024)S(1)}, f32[2048]{0:T(1024)S(1)}, f32[2048]{0:T(1024)S(1)}, f32[2048]{0:T(1024)S(1)}, /*index=5*/f32[2048]{0:T(1024)S(1)}) fusion(f32[2048]{0:T(1024)S(1)} %bitcast.267, f32[1024]{0:T(1024)S(1)} %bitcast.279, f32[2048]{0:T(1024)S(1)} %bitcast.264, f32[1024]{0:T(1024)S(1)} %bitcast.282, ...), kind=kLoop, calls=%fused_computation.85.clone.1 | loop fusion | flops 85970944 | bytes 122880 | tf_op jit(solution)/shard_map/while/body/eval_jaxpr/reduce_sum | solution.py:28
  739.3 16.2 %fusion.66 = (f32[2048]{0:T(1024)S(1)}, f32[2048]{0:T(1024)S(1)}, f32[2048]{0:T(1024)S(1)}, f32[2048]{0:T(1024)S(1)}, f32[2048]{0:T(1024)S(1)}, /*index=5*/f32[2048]{0:T(1024)S(1)}) fusion(f32[2048]{0:T(1024)S(1)} %bitcast.267, f32[1024]{0:T(1024)S(1)} %bitcast.279, f32[2048]{0:T(1024)S(1)} %bitcast.264, f32[1024]{0:T(1024)S(1)} %bitcast.282, ...), kind=kLoop, calls=%fused_computation.85.clone.1 | loop fusion | flops 85970944 | bytes 122880 | tf_op jit(solution)/shard_map/while/body/eval_jaxpr/reduce_sum | solution.py:28
  756.8 16.2 %fusion.66 = (f32[2048]{0:T(1024)S(1)}, f32[2048]{0:T(1024)S(1)}, f32[2048]{0:T(1024)S(1)}, f32[2048]{0:T(1024)S(1)}, f32[2048]{0:T(1024)S(1)}, /*index=5*/f32[2048]{0:T(1024)S(1)}) fusion(f32[2048]{0:T(1024)S(1)} %bitcast.267, f32[1024]{0:T(1024)S(1)} %bitcast.279, f32[2048]{0:T(1024)S(1)} %bitcast.264, f32[1024]{0:T(1024)S(1)} %bitcast.282, ...), kind=kLoop, calls=%fused_computation.85.clone.1 | loop fusion | flops 85970944 | bytes 122880 | tf_op jit(solution)/shard_map/while/body/eval_jaxpr/reduce_sum | solution.py:28
  774.4 16.2 %fusion.66 = (f32[2048]{0:T(1024)S(1)}, f32[2048]{0:T(1024)S(1)}, f32[2048]{0:T(1024)S(1)}, f32[2048]{0:T(1024)S(1)}, f32[2048]{0:T(1024)S(1)}, /*index=5*/f32[2048]{0:T(1024)S(1)}) fusion(f32[2048]{0:T(1024)S(1)} %bitcast.267, f32[1024]{0:T(1024)S(1)} %bitcast.279, f32[2048]{0:T(1024)S(1)} %bitcast.264, f32[1024]{0:T(1024)S(1)} %bitcast.282, ...), kind=kLoop, calls=%fused_computation.85.clone.1 | loop fusion | flops 85970944 | bytes 122880 | tf_op jit(solution)/shard_map/while/body/eval_jaxpr/reduce_sum | solution.py:28
  796.4 138.7 %all-reduce.5.cloned.1.call-done = f32[6,32768]{1,0:T(8,128)} async-done(((f32[6,32768]{1,0:T(8,128)}), f32[6,32768]{1,0:T(8,128)}) %all-reduce.5.cloned.1.call-update) | async-done | bytes 786448 | tf_op jit(solution)/shard_map/psum | solution.py:83
  (235 shorter events, 199.8 us)
Async XLA Ops:
  14.2 12.9 %copy-start.3 = (f32[3,1024]{1,0:T(4,128)S(1)}, f32[3,1024]{1,0:T(4,128)}, u32[]{:S(2)}) copy-start(f32[3,1024]{1,0:T(4,128)} %param.11) | copy-start | bytes 36868
  15.5 11.8 %copy-start.4 = (f32[3,1024]{1,0:T(4,128)S(1)}, f32[3,1024]{1,0:T(4,128)}, u32[]{:S(2)}) copy-start(f32[3,1024]{1,0:T(4,128)} %param.12) | copy-start | bytes 36868
  15.5 12.0 %copy-start.5 = (f32[3,1024]{1,0:T(4,128)S(1)}, f32[3,1024]{1,0:T(4,128)}, u32[]{:S(2)}) copy-start(f32[3,1024]{1,0:T(4,128)} %param.13) | copy-start | bytes 36868
  15.5 28.1 %all-to-all-start = ((f32[128,1,6,256]{3,1,2,0:T(1,128)}), f32[128,1,6,256]{3,1,2,0:T(1,128)S(1)}, u32[]{:S(2)}, u32[]{:S(2)}) async-start(f32[128,1,6,256]{3,1,2,0:T(1,128)} %stack.48), calls=%async_computation | async-start | bytes 1572864 | tf_op jit(solution)/shard_map/all_to_all | solution.py:79
  27.0 0.8 copy-start.6
  27.0 445.4 %all-reduce.3.cloned.1.call-start = ((), (), s32[]{:S(2)}) async-start(), calls=%async_computation.2 | async-start | bytes 2097152 | tf_op jit(solution)/shard_map/psum | solution.py:83
  327.9 1.0 copy-start.1
  479.9 2.9 copy-start.2
  482.8 23.4 %all-to-all-start.1 = ((f32[128,1,6,256]{3,1,2,0:T(1,128)}), f32[128,1,6,256]{3,1,2,0:T(1,128)S(1)}, u32[]{:S(2)}, u32[]{:S(2)}) async-start(f32[128,1,6,256]{3,1,2,0:T(1,128)} %stack.49), calls=%async_computation.1 | async-start | bytes 1572864 | tf_op jit(solution)/shard_map/all_to_all | solution.py:79
  489.6 445.6 %all-reduce.5.cloned.1.call-start = ((), (), s32[]{:S(2)}) async-start(), calls=%async_computation.3 | async-start | bytes 2097152 | tf_op jit(solution)/shard_map/psum | solution.py:83
  790.7 1.0 copy-start
Sparse Core Ops, SparseCore 0:
  329.1 143.2 all-reduce.2
  791.9 143.2 all-reduce.4
